TPU v7x, 512 devices: a whole 4x8x8 slice. The times are simulated.
512 devices in a mesh: ctx: 16 (over y, x_hi), tp: 32 (over z, x_lo, core).
Axes of the slice: x: 4 (x_hi: 2, x_lo: 2; x = x_hi * 2 + x_lo), y: 8, z: 8, core: 2. Of those that a mesh axis runs over, the one named last changes fastest.
Arguments:
- resid_in: bfloat16 [2048, 4096], P('ctx', 'tp'), may hold values from -6 to 6
- feats: bfloat16 [2048, 3, 4096], P('ctx', None, 'tp'), may hold values from -6 to 6
- short_filter: float32 [3, 3, 4096], P(None, None, 'tp'), may hold values from -3.5 to 3.5
- residues: float32 [4096, 16], P('tp'), may hold values from -4 to 4
- rates: float32 [4096, 16], P('tp'), may hold values from 0.00014648438 to 0.03
- out_weight: bfloat16 [4096, 4096], P('tp'), may hold values from -0.1875 to 0.1875
- norm_gain: float32 [4096], replicated, may hold values from 0.1 to 1.9
- attn_weight: bfloat16 [4096, 3, 4096], P(None, None, 'tp'), may hold values from -1 to 1
Outputs:
- hyena_out: bfloat16 [2048, 4096], P('ctx', 'tp')
- context: bfloat16 [2048, 4096], P('ctx', 'tp')
All inputs are finite; a program needn't handle non-finite values.
Results may differ from a plain program's by a relative error of at most 0.01.
Values may be sent and summed in bfloat16 or wider, within the bound.
No kernel may reach another device: no remote copies, remote signals or barrier semaphores. Data moves between devices by JAX's collectives and lax.ppermute only.
A program may use at most 192 MiB of HBM per device.

v0:
```python
import math
import jax
import jax.numpy as jnp
from jax import lax
from jax.sharding import PartitionSpec as P

HEAD_DIM = 128
eps_norm = 1e-05
rope_base = 10000.0
mask_fill = -1e30
highest = lax.Precision.HIGHEST


def shifted(value, axis, steps):
    count = lax.axis_size(axis)
    initial, last = (max(0, -steps), min(count, count - steps))
    return lax.ppermute(value, axis, [(source, source + steps) for source in range(initial, last)])


def toeplitz_lower(filter_taps):
    chan_count, block_size = filter_taps.shape
    padded = jnp.concatenate(
        [jnp.zeros((chan_count, block_size - 1), jnp.float32), filter_taps], axis=1
    )
    flipped = padded[:, ::-1]
    tiled = jnp.tile(flipped, (1, block_size))
    offset = block_size - 1
    window = tiled[:, offset : offset + block_size * (2 * block_size - 2)]
    return window.reshape(chan_count, block_size, 2 * block_size - 2)[:, :, :block_size]


def modal_conv(signal, residues, rates, start_state):
    chan_count, length = signal.shape
    block_size = math.gcd(length, 128)
    block_count = length // block_size
    weight = residues * jnp.sqrt(1.0 - jnp.exp(-2.0 * rates))
    lag_steps = jnp.arange(block_size, dtype=jnp.float32)
    powers = jnp.exp(-rates[:, :, None] * lag_steps)
    filter_taps = jnp.sum(weight[:, :, None] * powers, axis=1)
    toeplitz = toeplitz_lower(filter_taps)
    blocks = signal.reshape(chan_count, block_count, block_size)
    inner_part = jnp.einsum("cij,cnj->cni", toeplitz, blocks, precision=highest)
    tail_powers = jnp.exp(-rates[:, :, None] * (block_size - lag_steps))
    end_states = jnp.einsum("cnj,cmj->cnm", blocks, tail_powers, precision=highest)
    block_steps = jnp.arange(block_count, dtype=jnp.float32)
    gap_count = block_steps[:, None] - 1.0 - block_steps[None, :]
    live_mask = gap_count >= 0.0
    carry_mat = jnp.where(
        live_mask, jnp.exp(-rates[:, :, None, None] * block_size * jnp.maximum(gap_count, 0.0)), 0.0
    )
    states = jnp.einsum("cmnk,ckm->cnm", carry_mat, end_states, precision=highest)
    states = (
        states
        + jnp.exp(-rates[:, None, :] * block_size * block_steps[None, :, None])
        * start_state[:, None, :]
    )
    cross_part = jnp.einsum("cnm,cmi->cni", states * weight[:, None, :], powers, precision=highest)
    return (inner_part + cross_part).reshape(chan_count, length)


def short_mix(feats, short_filter):
    row_count = feats.shape[0]
    prior_feats = shifted(feats[-2:], "ctx", 1)
    joined = jnp.concatenate([prior_feats, feats], axis=0).astype(jnp.float32)
    return (
        short_filter[0] * joined[2:]
        + short_filter[1] * joined[1 : row_count + 1]
        + short_filter[2] * joined[:row_count]
    )


def rotary_turn(vectors, positions):
    half_dim = vectors.shape[-1] // 2
    frequency = rope_base ** (-jnp.arange(half_dim, dtype=jnp.float32) * 2.0 / vectors.shape[-1])
    angles = positions.astype(jnp.float32)[:, None] * frequency[None, :]
    cosine = jnp.cos(angles)[:, None, :]
    sine_part = jnp.sin(angles)[:, None, :]
    first_half = vectors[..., :half_dim]
    second = vectors[..., half_dim:]
    return jnp.concatenate(
        [first_half * cosine - second * sine_part, second * cosine + first_half * sine_part],
        axis=-1,
    )


def attend_tile(running, query_rows, query_pos, key_block, value_block, key_start):
    run_peak, denom, accumulated = running
    block_size = key_block.shape[0]
    score_scale = 1.0 / math.sqrt(key_block.shape[2])
    key_pos = key_start + jnp.arange(block_size, dtype=jnp.int32)
    scores = (
        jnp.einsum("shd,khd->hsk", query_rows, key_block, preferred_element_type=jnp.float32)
        * score_scale
    )
    allowed = (query_pos[:, None] >= key_pos[None, :])[None]
    masked = jnp.where(allowed, scores, mask_fill)
    new_peak = jnp.maximum(run_peak, jnp.max(masked, axis=2))
    weights = jnp.where(allowed, jnp.exp(masked - new_peak[:, :, None]), 0.0)
    factor = jnp.exp(run_peak - new_peak)
    denom = denom * factor + jnp.sum(weights, axis=2)
    accumulated = accumulated * factor[:, :, None] + jnp.einsum(
        "hsk,khd->hsd",
        weights.astype(jnp.bfloat16),
        value_block,
        preferred_element_type=jnp.float32,
    )
    return (new_peak, denom, accumulated)


def empty_state(head_count, rows):
    return (
        jnp.full((head_count, rows), mask_fill, jnp.float32),
        jnp.zeros((head_count, rows), jnp.float32),
        jnp.zeros((head_count, rows, HEAD_DIM), jnp.float32),
    )


def finish_rows(state):
    run_peak, denom, accumulated = state
    heads_out = accumulated / denom[:, :, None]
    rows = heads_out.shape[1]
    return (
        heads_out.transpose(1, 0, 2)
        .reshape(rows, heads_out.shape[0] * heads_out.shape[2])
        .astype(jnp.bfloat16)
    )


def per_device(resid_in, feats, short_filter, residues, rates, out_weight, norm_gain, attn_weight):
    row_count, chan_count = resid_in.shape
    width_all = out_weight.shape[1]
    short_out = short_mix(feats, short_filter)
    product = (short_out[:, 1] * short_out[:, 2]).astype(jnp.bfloat16)
    panel_rows = lax.all_to_all(product.T, "ctx", split_axis=0, concat_axis=1, tiled=True)
    panel_count = chan_count // lax.axis_size("ctx")
    panel_start = lax.axis_index("ctx") * panel_count
    panel_res = lax.dynamic_slice_in_dim(residues, panel_start, panel_count, 0)
    panel_rates = lax.dynamic_slice_in_dim(rates, panel_start, panel_count, 0)
    panel_conv = modal_conv(
        panel_rows.astype(jnp.float32), panel_res, panel_rates, jnp.zeros_like(panel_rates)
    )
    returned = lax.all_to_all(panel_conv, "ctx", split_axis=1, concat_axis=0, tiled=True)
    conv_out = returned.T
    gated = (short_out[:, 0] * conv_out).astype(jnp.bfloat16)
    own_share = lax.psum_scatter(
        lax.dot_general(
            out_weight, gated, (((0,), (1,)), ((), ())), preferred_element_type=jnp.float32
        ),
        "tp",
        scatter_dimension=0,
        tiled=True,
    )
    hyena_out = (resid_in.astype(jnp.float32) + own_share.T).astype(jnp.bfloat16)
    full_rows = lax.all_gather(hyena_out, "tp", axis=1, tiled=True)
    wide = full_rows.astype(jnp.float32)
    mean_square = jnp.mean(wide * wide, axis=1, keepdims=True)
    normed = (wide * lax.rsqrt(mean_square + eps_norm) * norm_gain).astype(jnp.bfloat16)
    projected = jnp.dot(
        normed, attn_weight.reshape(width_all, 3 * chan_count), preferred_element_type=jnp.float32
    ).reshape(row_count, 3, chan_count)
    head_count = chan_count // HEAD_DIM
    ctx_index = lax.axis_index("ctx")
    first_pos = ctx_index * row_count
    positions = first_pos + jnp.arange(row_count, dtype=jnp.int32)
    queries = rotary_turn(
        projected[:, 0].reshape(row_count, head_count, HEAD_DIM), positions
    ).astype(jnp.bfloat16)
    keys_all = rotary_turn(
        projected[:, 1].reshape(row_count, head_count, HEAD_DIM), positions
    ).astype(jnp.bfloat16)
    values = projected[:, 2].astype(jnp.bfloat16)
    key_pieces = (keys_all.reshape(row_count, chan_count), values)
    initial = empty_state(head_count, row_count)
    key_rows = lax.all_gather(key_pieces[0], "ctx", axis=0, tiled=True)
    value_rows = lax.all_gather(key_pieces[1], "ctx", axis=0, tiled=True)
    key_total = key_rows.shape[0]
    tiles_block_size = math.gcd(key_total, 1024)
    block_count = key_total // tiles_block_size
    key_blocks = key_rows.reshape(block_count, tiles_block_size, head_count, HEAD_DIM)
    value_blocks = value_rows.reshape(block_count, tiles_block_size, head_count, HEAD_DIM)
    key_blocks, value_blocks, block_ids, block_size = (
        key_blocks,
        value_blocks,
        jnp.arange(block_count, dtype=jnp.int32),
        tiles_block_size,
    )

    def one_tile(carried, slot_item):
        key_block, value_block, block_index = slot_item
        key_start = block_index * block_size
        updated = attend_tile(carried, queries, positions, key_block, value_block, key_start)
        return (updated, None)

    result, _ = lax.scan(one_tile, initial, (key_blocks, value_blocks, block_ids))
    context = finish_rows(result)
    return (hyena_out, context)


def solution(mesh):
    in_specs = (
        P("ctx", "tp"),
        P("ctx", None, "tp"),
        P(None, None, "tp"),
        P("tp", None),
        P("tp", None),
        P("tp", None),
        P(),
        P(None, None, "tp"),
    )
    out_specs = (P("ctx", "tp"), P("ctx", "tp"))
    return jax.shard_map(
        per_device, mesh=mesh, in_specs=in_specs, out_specs=out_specs, check_vma=False
    )
```

profile of v0, /device:TPU:4, one launch (start us, length us, event | category | flops | bytes accessed | tf_op | source)
XLA Modules:
  0.0 341.5 jit_solution(16704651836069771264)
XLA Ops:
  7.2 0.0 copy-start
  7.2 0.8 slice.59
  8.0 0.2 copy.44
  8.1 3.4 %collective-permute-start = (bf16[2,3,128]{0,2,1:T(8,128)(2,1)S(1)}, bf16[2,3,128]{0,2,1:T(8,128)(2,1)S(1)}, u32[]{:S(2)}, u32[]{:S(2)}) collective-permute-start(bf16[2,3,128]{0,2,1:T(8,128)(2,1)S(1)} %copy.44), channel_id=1, source_target_pairs={{0,32},{32,64},{64,96},{96,128},{128,160},{160,192},{192,224},{224... | collective-permute-start | bytes 4616 | tf_op jit(solution)/shard_map/ppermute | solution.py:17
  11.6 0.1 fusion.79
  11.7 0.1 fusion.80
  11.8 0.8 constant_dynamic-slice_fusion
  12.5 0.1 copy.63
  12.6 0.1 copy.64
  12.7 0.7 slice_bitcast_fusion.3
  13.4 0.1 multiply_reduce_fusion.1
  13.5 1.0 copy.45
  14.5 0.1 concatenate.30
  14.6 0.1 reverse
  14.8 0.1 slice.135
  14.8 0.1 tile.4
  14.9 0.6 tile.10
  15.5 0.3 slice.81
  15.9 1.6 reshape.257
  17.5 0.4 collective-permute-done
  17.9 0.1 maximum_convert_fusion
  18.0 0.3 fusion.34
  18.4 0.6 fusion.65
  19.0 8.8 %all-to-all-start = ((bf16[16,8,128]{2,1,0:T(8,128)(2,1)}), bf16[16,8,128]{2,1,0:T(8,128)(2,1)S(1)}, u32[]{:S(2)}, u32[]{:S(2)}) async-start(bf16[16,8,128]{2,1,0:T(8,128)(2,1)} %fusion.65), calls=%async_computation | async-start | bytes 65536 | tf_op jit(solution)/shard_map/all_to_all | solution.py:134
  27.8 0.0 reduce-scatter.2.cloned.1.call-start
  27.8 7.4 %all-to-all-done = bf16[16,8,128]{2,1,0:T(8,128)(2,1)S(1)} async-done(((bf16[16,8,128]{2,1,0:T(8,128)(2,1)}), bf16[16,8,128]{2,1,0:T(8,128)(2,1)S(1)}, u32[]{:S(2)}, u32[]{:S(2)}) %all-to-all-start) | async-done | bytes 32800 | tf_op jit(solution)/shard_map/all_to_all | solution.py:134
  35.2 0.2 convolution_bitcast_fusion.2
  35.5 0.1 copy.65
  35.5 0.6 multiply_reduce_fusion
  36.1 0.1 copy.60
  36.2 0.5 fusion.32
  36.7 0.3 convolution_add_fusion
  37.0 13.1 %all_to_all.32 = f32[8,16,128]{2,0,1:T(8,128)S(1)} all-to-all(f32[8,16,128]{2,0,1:T(8,128)S(1)} %copy.49), channel_id=1, replica_groups=mesh['ctx'=16,'tp'=32] {'ctx'}, dimensions={1} | all-to-all | bytes 131072 | tf_op jit(solution)/shard_map/all_to_all | solution.py:142
  50.2 0.0 copy-done
  50.2 0.0 copy-start.1
  50.2 1.8 convolution_bitcast_fusion.1
  52.0 0.0 reduce-scatter.2.cloned.1.call-update
  52.0 0.0 all-gather.3.cloned.1.call-start
  52.1 122.4 %reduce-scatter.2.cloned.1.call-done = f32[128,128]{0,1:T(8,128)} async-done(((f32[4096,128]{0,1:T(8,128)}), f32[128,128]{0,1:T(8,128)}) %reduce-scatter.2.cloned.1.call-update) | async-done | bytes 65552 | tf_op jit(solution)/shard_map/reduce_scatter | solution.py:145
  174.4 0.0 copy-done.1
  174.4 1.5 fusion.39
  175.9 0.0 all-gather.3.cloned.1.call-update
  175.9 0.0 copy-start.2
  176.0 4.7 %copy.50 = bf16[4096,3,128]{0,2,1:T(8,128)(2,1)} copy(bf16[4096,3,128]{2,0,1:T(8,128)(2,1)} %param.17) | data formatting | bytes 6291456 | tf_op args[7]
  180.7 59.4 %all-gather.3.cloned.1.call-done = bf16[128,4096]{1,0:T(8,128)(2,1)} async-done(((bf16[128,128]{1,0:T(8,128)(2,1)}), bf16[128,4096]{1,0:T(8,128)(2,1)}) %all-gather.3.cloned.1.call-update) | async-done | bytes 1048592 | tf_op jit(solution)/shard_map/all_gather | solution.py:154
  240.1 1.5 fusion.25
  241.6 0.0 copy-done.2
  241.6 3.3 fusion.23
  244.9 0.2 fusion.61
  245.1 0.1 copy.52
  245.3 39.5 %all_gather.10 = bf16[2048,128]{0,1:T(8,128)(2,1)S(1)} all-gather(bf16[128,128]{0,1:T(8,128)(2,1)S(1)} %pad_maximum_fusion), channel_id=1, replica_groups=mesh['ctx'=16,'tp'=32] {'ctx'}, dimensions={0}, use_global_device_ids=true | all-gather | bytes 557056 | tf_op jit(solution)/shard_map/all_gather | solution.py:174
  284.7 0.3 copy.61
  285.0 44.0 %all-gather = bf16[2048,1,128]{0,2,1:T(8,128)(2,1)S(1)} all-gather(bf16[128,1,128]{0,2,1:T(8,128)(2,1)S(1)} %slice.136), channel_id=2, replica_groups=mesh['ctx'=16,'tp'=32] {'ctx'}, dimensions={0}, use_global_device_ids=true | all-gather | bytes 557056 | tf_op jit(solution)/shard_map/all_gather | solution.py:175
  329.0 0.3 copy.62
  329.3 4.6 %while.15 = (s32[]{:T(128)}, f32[1,128]{1,0:T(1,128)S(1)}, f32[1,128]{1,0:T(1,128)S(1)}, f32[1,128,128]{2,1,0:T(8,128)S(1)}, s32[2]{0:T(128)S(1)}, /*index=5*/bf...) while((s32[]{:T(128)}, f32[1,128]{1,0:T(1,128)S(1)}, ...), condition=%wide.region_6.7_spmd.clone, body=%wide.region_3.6_spmd.clone.sunk | while | flops 68732800 | bytes 2287785 | solution.py:194
  329.3 0.6 dynamic_slice.39
  330.6 0.3 fusion.93
  330.9 0.4 fusion.97
  331.4 0.2 fusion.95
  331.6 0.6 dynamic_slice.39
  332.9 0.3 fusion.93
  333.3 0.4 fusion.97
  333.7 0.2 fusion.95
  333.9 0.7 fusion.74
  (24 shorter events, 0.2 us)
Async XLA Ops:
  7.2 43.0 %copy-start = (bf16[128,4096]{1,0:T(8,128)(2,1)S(1)}, bf16[128,4096]{1,0:T(8,128)(2,1)}, u32[]{:S(2)}) copy-start(bf16[128,4096]{1,0:T(8,128)(2,1)} %param.15) | copy-start | bytes 3145732
  8.1 9.7 %collective-permute-start = (bf16[2,3,128]{0,2,1:T(8,128)(2,1)S(1)}, bf16[2,3,128]{0,2,1:T(8,128)(2,1)S(1)}, u32[]{:S(2)}, u32[]{:S(2)}) collective-permute-start(bf16[2,3,128]{0,2,1:T(8,128)(2,1)S(1)} %copy.44), channel_id=1, source_target_pairs={{0,32},{32,64},{64,96},{96,128},{128,160},{160,192},{192,224},{224... | collective-permute-start | bytes 4616 | tf_op jit(solution)/shard_map/ppermute | solution.py:17
  19.0 16.2 %all-to-all-start = ((bf16[16,8,128]{2,1,0:T(8,128)(2,1)}), bf16[16,8,128]{2,1,0:T(8,128)(2,1)S(1)}, u32[]{:S(2)}, u32[]{:S(2)}) async-start(bf16[16,8,128]{2,1,0:T(8,128)(2,1)} %fusion.65), calls=%async_computation | async-start | bytes 65536 | tf_op jit(solution)/shard_map/all_to_all | solution.py:134
  27.8 146.7 %reduce-scatter.2.cloned.1.call-start = ((), (), s32[]{:S(2)}) async-start(), calls=%async_computation.3 | async-start | bytes 2162688 | tf_op jit(solution)/shard_map/reduce_scatter | solution.py:145
  50.2 124.3 %copy-start.1 = (bf16[128,128]{1,0:T(8,128)(2,1)S(1)}, bf16[128,128]{1,0:T(8,128)(2,1)}, u32[]{:S(2)}) copy-start(bf16[128,128]{1,0:T(8,128)(2,1)} %param.10) | copy-start | bytes 98308
  52.0 188.1 %all-gather.3.cloned.1.call-start = ((), (), s32[]{:S(2)}) async-start(), calls=%async_computation.4 | async-start | bytes 1081344 | tf_op jit(solution)/shard_map/all_gather | solution.py:154
  175.9 65.7 %copy-start.2 = (f32[4096]{0:T(1024)S(1)}, f32[4096]{0:T(1024)}, u32[]{:S(2)}) copy-start(f32[4096]{0:T(1024)} %param.16) | copy-start | bytes 49156
Sparse Core Ops, SparseCore 0:
  52.1 122.2 reduce-scatter.1
  177.3 62.7 all-gather.2
where the time goes:
time: 342 us; the launch traced here: 341 us
  waiting for transfers between devices  190 us (56%)
  blocking collectives  96.6 us (28%)
  between operations  14.3 us (4%)
  local copies, waits for them, and re-layouts  13.3 us (4%)
  starting transfers between devices  12.3 us (4%)
  matrix products  7.62 us (2%)
  other arithmetic  6.38 us (2%)
    reduce_scatter x1, waiting for transfers between devices, per_device(): lax.psum_scatter(lax.dot_general(out_weight, gated, (((0,), (1,)), ((), (...  122 us
    all_gather x1, waiting for transfers between devices, per_device(): full_rows = lax.all_gather(hyena_out, 'tp', axis=1, tiled=True)  59.4 us
    all_gather x1, blocking collectives, per_device(): value_rows = lax.all_gather(key_pieces[1], 'ctx', axis=0, tiled=True)  44 us
    all_gather x1, blocking collectives, per_device(): key_rows = lax.all_gather(key_pieces[0], 'ctx', axis=0, tiled=True)  39.5 us
    all_to_all x1, blocking collectives, per_device(): lax.all_to_all(panel_conv, 'ctx', split_axis=1, concat_axis=0, tiled=True)  13.1 us
    all_to_all x1, starting transfers between devices, per_device(): lax.all_to_all(product.T, 'ctx', split_axis=0, concat_axis=1, tiled=True)  8.78 us
    all_to_all x1, waiting for transfers between devices, per_device(): lax.all_to_all(product.T, 'ctx', split_axis=0, concat_axis=1, tiled=True)  7.39 us
  transfers between devices with their start and end apart: 4, of which 4 were waited for; matrix products, arithmetic and copies ran while one was open for 3% of the time, Pallas kernels for 0%

commit v1 on v0

--- a/solution.py
+++ b/solution.py
@@ -171,7 +171,9 @@
     values = projected[:, 2].astype(jnp.bfloat16)
     key_pieces = (keys_all.reshape(row_count, chan_count), values)
     initial = empty_state(head_count, row_count)
-    key_rows = lax.all_gather(key_pieces[0], "ctx", axis=0, tiled=True)
+    block = key_pieces[0]
+    sent = jnp.stack([block] * lax.axis_size("ctx"))
+    key_rows = jnp.concatenate(lax.all_to_all(sent, "ctx", 0, 0), axis=0)
     value_rows = lax.all_gather(key_pieces[1], "ctx", axis=0, tiled=True)
     key_total = key_rows.shape[0]
     tiles_block_size = math.gcd(key_total, 1024)

time: 342 us -> 317 us (0.927)
  the two profiles are of different devices: /device:TPU:4 before, /device:TPU:32 now
where the time goes in v1:
time: 317 us
  waiting for transfers between devices  189 us (60%)
  blocking collectives  62 us (20%)
  starting transfers between devices  21.8 us (7%)
  between operations  14.3 us (5%)
  local copies, waits for them, and re-layouts  14.1 us (4%)
  matrix products  7.61 us (2%)
  other arithmetic  6.38 us (2%)
    reduce_scatter x1, waiting for transfers between devices, per_device(): lax.psum_scatter(lax.dot_general(out_weight, gated, (((0,), (1,)), ((), (...  125 us
    all_gather x1, waiting for transfers between devices, per_device(): full_rows = lax.all_gather(hyena_out, 'tp', axis=1, tiled=True)  59.5 us
    all_gather x1, blocking collectives, per_device(): value_rows = lax.all_gather(key_pieces[1], 'ctx', axis=0, tiled=True)  48.8 us
    all_to_all x1, blocking collectives, per_device(): lax.all_to_all(panel_conv, 'ctx', split_axis=1, concat_axis=0, tiled=True)  13.2 us
    all_to_all x1, starting transfers between devices, per_device(): key_rows = jnp.concatenate(lax.all_to_all(sent, 'ctx', 0, 0), axis=0)  9.51 us
    all_to_all x1, starting transfers between devices, per_device(): lax.all_to_all(product.T, 'ctx', split_axis=0, concat_axis=1, tiled=True)  7.28 us
    unnamed x15, local copies, waits for them, and re-layouts  6.55 us
  transfers between devices with their start and end apart: 5, of which 3 were waited for; matrix products, arithmetic and copies ran while one was open for 3% of the time, Pallas kernels for 0%

profile of v1, /device:TPU:32, one launch (start us, length us, event | category | flops | bytes accessed | tf_op | source)
XLA Modules:
  0.0 316.8 jit_solution(1004326427091582723)
XLA Ops:
  7.2 0.0 copy-start
  7.2 0.8 slice.59
  8.0 0.2 copy.46
  8.1 4.9 %collective-permute-start = (bf16[2,3,128]{0,2,1:T(8,128)(2,1)S(1)}, bf16[2,3,128]{0,2,1:T(8,128)(2,1)S(1)}, u32[]{:S(2)}, u32[]{:S(2)}) collective-permute-start(bf16[2,3,128]{0,2,1:T(8,128)(2,1)S(1)} %copy.46), channel_id=1, source_target_pairs={{0,32},{32,64},{64,96},{96,128},{128,160},{160,192},{192,224},{224... | collective-permute-start | bytes 4616 | tf_op jit(solution)/shard_map/ppermute | solution.py:17
  13.1 0.1 fusion.79
  13.2 0.1 fusion.80
  13.3 0.8 constant_dynamic-slice_fusion
  14.0 0.1 copy.65
  14.1 0.1 copy.66
  14.2 0.7 slice_bitcast_fusion.3
  14.9 0.1 multiply_reduce_fusion.1
  15.0 1.0 copy.47
  16.0 0.1 concatenate.31
  16.1 0.1 reverse
  16.3 0.1 slice.135
  16.3 0.1 tile.4
  16.4 0.6 tile.10
  17.0 0.3 slice.81
  17.4 1.6 reshape.258
  19.0 0.0 collective-permute-done
  19.0 0.1 maximum_convert_fusion
  19.1 0.3 fusion.34
  19.5 0.6 fusion.65
  20.1 7.3 %all-to-all-start = ((bf16[16,8,128]{2,1,0:T(8,128)(2,1)}), bf16[16,8,128]{2,1,0:T(8,128)(2,1)S(1)}, u32[]{:S(2)}, u32[]{:S(2)}) async-start(bf16[16,8,128]{2,1,0:T(8,128)(2,1)} %fusion.65), calls=%async_computation | async-start | bytes 65536 | tf_op jit(solution)/shard_map/all_to_all | solution.py:134
  27.4 0.0 reduce-scatter.2.cloned.1.call-start
  27.4 5.0 %all-to-all-done = bf16[16,8,128]{2,1,0:T(8,128)(2,1)S(1)} async-done(((bf16[16,8,128]{2,1,0:T(8,128)(2,1)}), bf16[16,8,128]{2,1,0:T(8,128)(2,1)S(1)}, u32[]{:S(2)}, u32[]{:S(2)}) %all-to-all-start) | async-done | bytes 32800 | tf_op jit(solution)/shard_map/all_to_all | solution.py:134
  32.4 0.2 convolution_bitcast_fusion.2
  32.7 0.1 copy.67
  32.8 0.6 multiply_reduce_fusion
  33.3 0.1 copy.63
  33.4 0.5 fusion.32
  33.9 0.3 convolution_add_fusion
  34.3 13.2 %all_to_all.37 = f32[8,16,128]{2,0,1:T(8,128)S(1)} all-to-all(f32[8,16,128]{2,0,1:T(8,128)S(1)} %copy.51), channel_id=1, replica_groups=mesh['ctx'=16,'tp'=32] {'ctx'}, dimensions={1} | all-to-all | bytes 131072 | tf_op jit(solution)/shard_map/all_to_all | solution.py:142
  47.5 0.0 copy-done
  47.5 1.8 convolution_bitcast_fusion.1
  49.2 0.0 reduce-scatter.2.cloned.1.call-update
  49.3 0.0 all-gather.3.cloned.1.call-start
  49.3 124.8 %reduce-scatter.2.cloned.1.call-done = f32[128,128]{0,1:T(8,128)} async-done(((f32[4096,128]{0,1:T(8,128)}), f32[128,128]{0,1:T(8,128)}) %reduce-scatter.2.cloned.1.call-update) | async-done | bytes 65552 | tf_op jit(solution)/shard_map/reduce_scatter | solution.py:145
  174.1 0.0 copy-done.1
  174.1 1.5 fusion.39
  175.6 0.0 all-gather.3.cloned.1.call-update
  175.6 0.0 copy-start.2
  175.6 4.7 %copy.52 = bf16[4096,3,128]{0,2,1:T(8,128)(2,1)} copy(bf16[4096,3,128]{2,0,1:T(8,128)(2,1)} %param.17) | data formatting | bytes 6291456 | tf_op args[7]
  180.3 59.5 %all-gather.3.cloned.1.call-done = bf16[128,4096]{1,0:T(8,128)(2,1)} async-done(((bf16[128,128]{1,0:T(8,128)(2,1)}), bf16[128,4096]{1,0:T(8,128)(2,1)}) %all-gather.3.cloned.1.call-update) | async-done | bytes 1048592 | tf_op jit(solution)/shard_map/all_gather | solution.py:154
  239.9 1.5 fusion.25
  241.4 3.3 %fusion.23 = f32[128,3,128]{0,2,1:T(8,128)S(1)} fusion(bf16[4096,3,128]{0,2,1:T(8,128)(2,1)} %copy.52, bf16[128,4096]{1,0:T(8,128)(2,1)} %all-gather.3.cloned.1.call-done, f32[4096]{0:T(1024)S(1)} %copy-done.2, f32[128]{0:T(128)S(1)} %add_rsqrt_fusion), kind=kOutput, calls=%fused_computation.32 | convolution fusion | flops 404750336 | bytes 4407808 | tf_op jit(solution)/shard_map/dot_general | solution.py:158
  244.7 0.2 fusion.61
  244.9 0.1 copy.53
  245.0 0.9 stack.3
  245.9 9.5 %all-to-all-start.2 = ((bf16[16,128,128]{2,1,0:T(8,128)(2,1)}), bf16[16,128,128]{2,1,0:T(8,128)(2,1)S(1)}, u32[]{:S(2)}, u32[]{:S(2)}) async-start(bf16[16,128,128]{2,1,0:T(8,128)(2,1)} %stack.3), calls=%async_computation.3 | async-start | bytes 1048576 | tf_op jit(solution)/shard_map/all_to_all | solution.py:176
  255.5 48.8 %all-gather = bf16[2048,1,128]{0,2,1:T(8,128)(2,1)S(1)} all-gather(bf16[128,1,128]{0,2,1:T(8,128)(2,1)S(1)} %slice.136), channel_id=2, replica_groups=mesh['ctx'=16,'tp'=32] {'ctx'}, dimensions={0}, use_global_device_ids=true | all-gather | bytes 557056 | tf_op jit(solution)/shard_map/all_gather | solution.py:177
  304.2 0.3 copy.64
  304.5 0.1 copy.55
  304.6 0.0 all-to-all-done.2
  304.7 4.6 %while.15 = (s32[]{:T(128)}, f32[1,128]{1,0:T(1,128)S(1)}, f32[1,128]{1,0:T(1,128)S(1)}, f32[1,128,128]{2,1,0:T(8,128)S(1)}, s32[2]{0:T(128)S(1)}, /*index=5*/bf...) while((s32[]{:T(128)}, f32[1,128]{1,0:T(1,128)S(1)}, ...), condition=%wide.region_6.7_spmd.clone, body=%wide.region_3.6_spmd.clone.sunk | while | flops 68732800 | bytes 2287785 | solution.py:196
  304.7 0.6 dynamic_slice.39
  305.9 0.3 fusion.93
  306.3 0.4 fusion.97
  306.7 0.2 fusion.95
  307.0 0.6 dynamic_slice.39
  308.2 0.3 fusion.93
  308.6 0.4 fusion.97
  309.0 0.2 fusion.95
  309.2 0.7 fusion.74
  (26 shorter events, 0.2 us)
Async XLA Ops:
  7.2 40.3 %copy-start = (bf16[128,4096]{1,0:T(8,128)(2,1)S(1)}, bf16[128,4096]{1,0:T(8,128)(2,1)}, u32[]{:S(2)}) copy-start(bf16[128,4096]{1,0:T(8,128)(2,1)} %param.15) | copy-start | bytes 3145732
  8.1 10.8 %collective-permute-start = (bf16[2,3,128]{0,2,1:T(8,128)(2,1)S(1)}, bf16[2,3,128]{0,2,1:T(8,128)(2,1)S(1)}, u32[]{:S(2)}, u32[]{:S(2)}) collective-permute-start(bf16[2,3,128]{0,2,1:T(8,128)(2,1)S(1)} %copy.46), channel_id=1, source_target_pairs={{0,32},{32,64},{64,96},{96,128},{128,160},{160,192},{192,224},{224... | collective-permute-start | bytes 4616 | tf_op jit(solution)/shard_map/ppermute | solution.py:17
  20.1 12.3 %all-to-all-start = ((bf16[16,8,128]{2,1,0:T(8,128)(2,1)}), bf16[16,8,128]{2,1,0:T(8,128)(2,1)S(1)}, u32[]{:S(2)}, u32[]{:S(2)}) async-start(bf16[16,8,128]{2,1,0:T(8,128)(2,1)} %fusion.65), calls=%async_computation | async-start | bytes 65536 | tf_op jit(solution)/shard_map/all_to_all | solution.py:134
  27.4 146.7 %reduce-scatter.2.cloned.1.call-start = ((), (), s32[]{:S(2)}) async-start(), calls=%async_computation.4 | async-start | bytes 2162688 | tf_op jit(solution)/shard_map/reduce_scatter | solution.py:145
  47.5 126.6 %copy-start.1 = (bf16[128,128]{1,0:T(8,128)(2,1)S(1)}, bf16[128,128]{1,0:T(8,128)(2,1)}, u32[]{:S(2)}) copy-start(bf16[128,128]{1,0:T(8,128)(2,1)} %param.10) | copy-start | bytes 98308
  49.3 190.6 %all-gather.3.cloned.1.call-start = ((), (), s32[]{:S(2)}) async-start(), calls=%async_computation.5 | async-start | bytes 1081344 | tf_op jit(solution)/shard_map/all_gather | solution.py:154
  175.6 65.8 %copy-start.2 = (f32[4096]{0:T(1024)S(1)}, f32[4096]{0:T(1024)}, u32[]{:S(2)}) copy-start(f32[4096]{0:T(1024)} %param.16) | copy-start | bytes 49156
  245.9 58.7 %all-to-all-start.2 = ((bf16[16,128,128]{2,1,0:T(8,128)(2,1)}), bf16[16,128,128]{2,1,0:T(8,128)(2,1)S(1)}, u32[]{:S(2)}, u32[]{:S(2)}) async-start(bf16[16,128,128]{2,1,0:T(8,128)(2,1)} %stack.3), calls=%async_computation.3 | async-start | bytes 1048576 | tf_op jit(solution)/shard_map/all_to_all | solution.py:176
Sparse Core Ops, SparseCore 0:
  49.4 124.6 reduce-scatter.1
  176.9 62.8 all-gather.2
